TPU v7x, 256 devices: a whole 4x4x8 slice. The times are simulated.
256 devices in a mesh: blk: 4 (over y_hi, core), reader: 8 (over y_lo, x), bulk: 8 (over z).
Axes of the slice: x: 4, y: 4 (y_hi: 2, y_lo: 2; y = y_hi * 2 + y_lo), z: 8, core: 2. Of those that a mesh axis runs over, the one named last changes fastest.
Arguments:
- vectors: float32 [128, 32768], P('bulk', ('blk', 'reader')), may hold values from -6 to 6
- ham_tiles: float32 [32, 4, 24, 128, 128], P(('blk', 'reader'))
- tile_rows: int32 [32, 4, 24], P(('blk', 'reader')), may hold values from 0 to 7, as said below
- tile_cols: int32 [32, 4, 24], P(('blk', 'reader')), may hold values from 0 to 63
- center: float32 [1], replicated, may hold values from -0.5 to 0.5
- halfwidth: float32 [1], replicated, may hold values from 1 to 2
Outputs:
- filtered: float32 [128, 32768], P('bulk', ('blk', 'reader'))
Inputs may be any that keep to these rules, and one draw needn't show every extreme that they name: tile_rows and tile_cols of one panel together name 24 different tiles.
All inputs are finite; a program needn't handle non-finite values.
Results may differ from a plain program's by a relative error of at most 0.0003.
Values sent between devices are 32-bit elements; how exact they have to be, the bound alone decides.
No kernel may reach another device: no remote copies, remote signals or barrier semaphores. Data moves between devices by JAX's collectives and lax.ppermute only.
A program may use at most 64 MiB of HBM per device.

v0:
```python
import jax
import jax.numpy as jnp
from jax import lax
from jax.sharding import PartitionSpec as P

TILE = 128
PASSES = 2


def contribute(sources, tiles, rows, count):
    product = jnp.einsum("vkc,krc->vkr", sources, tiles, precision=lax.Precision.HIGHEST)
    onehot = (rows[:, None] == jnp.arange(count, dtype=jnp.int32)[None, :]).astype(jnp.float32)
    return jnp.einsum("vkr,kt->vtr", product, onehot, precision=lax.Precision.HIGHEST)


def apply_ham(current, tiles_here, rows_here, cols_here):
    local_vecs = current.shape[0]
    row_tiles = current.shape[1] // TILE
    groups = tiles_here.shape[0]
    slots = tiles_here.shape[1]
    group_tiles = lax.axis_size("reader") * row_tiles
    whole = lax.all_gather(current, ("blk", "reader"), axis=1, tiled=True)
    tiled = whole.reshape(local_vecs, whole.shape[1] // TILE, TILE)
    offsets = (jnp.arange(groups, dtype=jnp.int32) * group_tiles)[:, None]
    glob = (offsets + cols_here).reshape(-1)
    sources = jnp.take(tiled, glob, axis=1)
    total = contribute(
        sources, tiles_here.reshape(groups * slots, TILE, TILE), rows_here.reshape(-1), row_tiles
    )
    return total.reshape(local_vecs, row_tiles * TILE)


def shards(vectors, ham_tiles, tile_rows, tile_cols, center, halfwidth):
    tiles_here = ham_tiles[0]
    rows_here = tile_rows[0]
    cols_here = tile_cols[0]
    total_rows = vectors.shape[1] * lax.axis_size("blk") * lax.axis_size("reader")

    def scaled(field):
        return (apply_ham(field, tiles_here, rows_here, cols_here) - center[0] * field) / halfwidth[
            0
        ]

    current = vectors
    for step in range(PASSES):
        first = scaled(current)
        second = 2.0 * scaled(first) - current
        third = 2.0 * scaled(second) - first
        squares = lax.psum(jnp.sum(third * third, axis=1), ("blk", "reader"))
        current = third / jnp.sqrt(squares / total_rows + 1e-06)[:, None]
    return current


def solution(mesh):
    return jax.shard_map(
        shards,
        mesh=mesh,
        in_specs=(
            P("bulk", ("blk", "reader")),
            P(("blk", "reader"), None, None, None, None),
            P(("blk", "reader"), None, None),
            P(("blk", "reader"), None, None),
            P(),
            P(),
        ),
        out_specs=P("bulk", ("blk", "reader")),
        check_vma=False,
    )
```

profile of v0, /device:TPU:32, one launch (start us, length us, event | category | flops | bytes accessed | tf_op | source)
XLA Modules:
  0.0 754.0 jit_solution(11329175917317144318)
XLA Ops:
  6.5 0.0 all-gather.7.cloned.1.call-start
  6.5 0.7 all-gather.7.cloned.1.call-update
  7.3 0.0 all-gather.9.cloned.1.call-start
  8.6 0.8 eq.8
  9.4 0.8 squeeze.6
  10.1 0.1 add.20
  10.2 0.1 add.21
  10.3 85.0 %all-gather.7.cloned.1.call-done = f32[16,32768]{1,0:T(8,128)} async-done(((f32[16,1024]{1,0:T(8,128)}), f32[16,32768]{1,0:T(8,128)}) %all-gather.7.cloned.1.call-update) | async-done | bytes 2097168 | tf_op jit(solution)/shard_map/all_gather | solution.py:22
  95.3 1.7 copy_bitcast_fusion.5
  97.1 0.7 gather_fusion
  97.8 0.0 copy-start.2
  97.8 12.0 %convolution_bitcast_fusion.5 = f32[16,96,128]{2,0,1:T(8,128)S(1)} fusion(f32[96,128,128]{2,1,0:T(8,128)} %bitcast.143, f32[96,16,128]{2,1,0:T(8,128)S(1)} %gather_fusion, pred[96]{0:T(512)(128)(4,1)S(1)} %get-tuple-element.10), kind=kOutput, calls=%fused_computation.17 | convolution fusion | flops 302186496 | bytes 7864416 | tf_op jit(solution)/shard_map/vkc,krc->vkr/dot_general | solution.py:11
  109.8 0.6 fusion.16
  110.3 0.0 copy-done.2
  110.3 0.6 fusion.49
  111.0 0.0 all-gather.9.cloned.1.call-update
  111.0 0.0 all-gather.11.cloned.1.call-start
  111.1 85.4 %all-gather.9.cloned.1.call-done = f32[16,32768]{1,0:T(8,128)} async-done(((f32[16,1024]{1,0:T(8,128)}), f32[16,32768]{1,0:T(8,128)}) %all-gather.9.cloned.1.call-update) | async-done | bytes 2097168 | tf_op jit(solution)/shard_map/all_gather | solution.py:22
  196.5 1.7 copy_bitcast_fusion.4
  198.3 0.7 gather_fusion.1
  199.0 0.0 copy-start.1
  199.0 12.0 %convolution_bitcast_fusion.4 = f32[16,96,128]{2,0,1:T(8,128)S(1)} fusion(f32[96,128,128]{2,1,0:T(8,128)} %bitcast.144, f32[96,16,128]{2,1,0:T(8,128)S(1)} %gather_fusion.1, pred[96]{0:T(512)(128)(4,1)S(1)} %get-tuple-element.10), kind=kOutput, calls=%fused_computation.16 | convolution fusion | flops 302186496 | bytes 7864416 | tf_op jit(solution)/shard_map/vkc,krc->vkr/dot_general | solution.py:11
  210.9 0.6 fusion.14
  211.5 0.0 copy-done.1
  211.5 0.7 fusion.48
  212.2 0.0 all-gather.11.cloned.1.call-update
  212.2 0.2 all-gather.13.cloned.1.call-start
  212.4 85.3 %all-gather.11.cloned.1.call-done = f32[16,32768]{1,0:T(8,128)} async-done(((f32[16,1024]{1,0:T(8,128)}), f32[16,32768]{1,0:T(8,128)}) %all-gather.11.cloned.1.call-update) | async-done | bytes 2097168 | tf_op jit(solution)/shard_map/all_gather | solution.py:22
  297.7 1.7 copy_bitcast_fusion.3
  299.4 0.7 gather_fusion.2
  300.1 0.0 copy-start.4
  300.1 12.0 %convolution_bitcast_fusion.3 = f32[16,96,128]{2,0,1:T(8,128)S(1)} fusion(f32[96,128,128]{2,1,0:T(8,128)} %bitcast.145, f32[96,16,128]{2,1,0:T(8,128)S(1)} %gather_fusion.2, pred[96]{0:T(512)(128)(4,1)S(1)} %get-tuple-element.10), kind=kOutput, calls=%fused_computation.15 | convolution fusion | flops 302186496 | bytes 7864416 | tf_op jit(solution)/shard_map/vkc,krc->vkr/dot_general | solution.py:11
  312.1 0.6 fusion.12
  312.7 0.0 copy-done.4
  312.7 0.1 multiply_reduce_fusion.1
  312.8 67.6 %psum.14 = f32[16]{0:T(128)S(1)} all-reduce(f32[16]{0:T(128)S(1)} %get-tuple-element.8), channel_id=1, replica_groups=mesh['blk'=4,'reader'=8,'bulk'=8] {'blk','reader'}, use_global_device_ids=true, to_apply=%region_1.3 | all-reduce | flops 16 | bytes 128 | tf_op jit(solution)/shard_map/psum | solution.py:49
  380.4 0.7 broadcast_divide_fusion.1
  381.1 0.0 all-gather.13.cloned.1.call-update
  381.1 0.0 all-gather.15.cloned.1.call-start
  381.2 80.1 %all-gather.13.cloned.1.call-done = f32[16,32768]{1,0:T(8,128)} async-done(((f32[16,1024]{1,0:T(8,128)}), f32[16,32768]{1,0:T(8,128)}) %all-gather.13.cloned.1.call-update) | async-done | bytes 2097168 | tf_op jit(solution)/shard_map/all_gather | solution.py:22
  461.2 1.7 copy_bitcast_fusion.2
  463.0 0.7 gather_fusion.3
  463.7 11.9 %convolution_bitcast_fusion.2 = f32[16,96,128]{2,0,1:T(8,128)S(1)} fusion(f32[96,128,128]{2,1,0:T(8,128)} %bitcast.146, f32[96,16,128]{2,1,0:T(8,128)S(1)} %gather_fusion.3, pred[96]{0:T(512)(128)(4,1)S(1)} %get-tuple-element.10), kind=kOutput, calls=%fused_computation.14 | convolution fusion | flops 302186496 | bytes 7864416 | tf_op jit(solution)/shard_map/vkc,krc->vkr/dot_general | solution.py:11
  475.6 0.6 fusion.10
  476.2 0.7 fusion.42
  476.9 0.0 all-gather.15.cloned.1.call-update
  476.9 0.3 all-gather.17.cloned.1.call-start
  477.2 85.2 %all-gather.15.cloned.1.call-done = f32[16,32768]{1,0:T(8,128)} async-done(((f32[16,1024]{1,0:T(8,128)}), f32[16,32768]{1,0:T(8,128)}) %all-gather.15.cloned.1.call-update) | async-done | bytes 2097168 | tf_op jit(solution)/shard_map/all_gather | solution.py:22
  562.4 1.7 copy_bitcast_fusion.1
  564.2 0.7 gather_fusion.4
  564.9 0.0 copy-start
  564.9 12.0 %convolution_bitcast_fusion.1 = f32[16,96,128]{2,0,1:T(8,128)S(1)} fusion(f32[96,128,128]{2,1,0:T(8,128)} %bitcast.147, f32[96,16,128]{2,1,0:T(8,128)S(1)} %gather_fusion.4, pred[96]{0:T(512)(128)(4,1)S(1)} %get-tuple-element.10), kind=kOutput, calls=%fused_computation.13 | convolution fusion | flops 302186496 | bytes 7864416 | tf_op jit(solution)/shard_map/vkc,krc->vkr/dot_general | solution.py:11
  576.9 0.6 fusion.8
  577.5 0.7 fusion.41
  578.2 0.0 all-gather.17.cloned.1.call-update
  578.2 85.5 %all-gather.17.cloned.1.call-done = f32[16,32768]{1,0:T(8,128)} async-done(((f32[16,1024]{1,0:T(8,128)}), f32[16,32768]{1,0:T(8,128)}) %all-gather.17.cloned.1.call-update) | async-done | bytes 2097168 | tf_op jit(solution)/shard_map/all_gather | solution.py:22
  663.7 1.7 copy_bitcast_fusion
  665.4 0.7 gather_fusion.5
  666.1 0.0 copy-start.3
  666.1 12.0 %convolution_bitcast_fusion = f32[16,96,128]{2,0,1:T(8,128)S(1)} fusion(f32[96,128,128]{2,1,0:T(8,128)} %bitcast.148, f32[96,16,128]{2,1,0:T(8,128)S(1)} %gather_fusion.5, pred[96]{0:T(512)(128)(4,1)S(1)} %get-tuple-element.10), kind=kOutput, calls=%fused_computation.12 | convolution fusion | flops 302186496 | bytes 7864416 | tf_op jit(solution)/shard_map/vkc,krc->vkr/dot_general | solution.py:11
  678.1 0.6 fusion.6
  678.7 0.1 multiply_reduce_fusion
  678.8 67.6 %psum.15 = f32[16]{0:T(128)S(1)} all-reduce(f32[16]{0:T(128)S(1)} %get-tuple-element.6), channel_id=1, replica_groups=mesh['blk'=4,'reader'=8,'bulk'=8] {'blk','reader'}, use_global_device_ids=true, to_apply=%region_3.5 | all-reduce | flops 16 | bytes 128 | tf_op jit(solution)/shard_map/psum | solution.py:49
  746.4 0.7 broadcast_divide_fusion
  (7 shorter events, 0.0 us)
Async XLA Ops:
  6.5 88.8 %all-gather.7.cloned.1.call-start = ((), (), s32[]{:S(2)}) async-start(), calls=%async_computation | async-start | bytes 2162688 | tf_op jit(solution)/shard_map/all_gather | solution.py:22
  7.3 189.2 %all-gather.9.cloned.1.call-start = ((), (), s32[]{:S(2)}) async-start(), calls=%async_computation.1 | async-start | bytes 2162688 | tf_op jit(solution)/shard_map/all_gather | solution.py:22
  97.8 12.6 %copy-start.2 = (f32[16,1024]{1,0:T(8,128)S(1)}, f32[16,1024]{1,0:T(8,128)}, u32[]{:S(2)}) copy-start(f32[16,1024]{1,0:T(8,128)} %param.8) | copy-start | bytes 196612
  111.0 186.7 %all-gather.11.cloned.1.call-start = ((), (), s32[]{:S(2)}) async-start(), calls=%async_computation.2 | async-start | bytes 2162688 | tf_op jit(solution)/shard_map/all_gather | solution.py:22
  199.0 12.6 %copy-start.1 = (f32[16,1024]{1,0:T(8,128)S(1)}, f32[16,1024]{1,0:T(8,128)}, u32[]{:S(2)}) copy-start(f32[16,1024]{1,0:T(8,128)} %fusion.49) | copy-start | bytes 196612
  212.2 249.0 %all-gather.13.cloned.1.call-start = ((), (), s32[]{:S(2)}) async-start(), calls=%async_computation.3 | async-start | bytes 2162688 | tf_op jit(solution)/shard_map/all_gather | solution.py:22
  300.1 12.6 %copy-start.4 = (f32[16,1024]{1,0:T(8,128)S(1)}, f32[16,1024]{1,0:T(8,128)}, u32[]{:S(2)}) copy-start(f32[16,1024]{1,0:T(8,128)} %fusion.48) | copy-start | bytes 196612
  381.1 181.3 %all-gather.15.cloned.1.call-start = ((), (), s32[]{:S(2)}) async-start(), calls=%async_computation.4 | async-start | bytes 2162688 | tf_op jit(solution)/shard_map/all_gather | solution.py:22
  476.9 186.7 %all-gather.17.cloned.1.call-start = ((), (), s32[]{:S(2)}) async-start(), calls=%async_computation.5 | async-start | bytes 2162688 | tf_op jit(solution)/shard_map/all_gather | solution.py:22
  564.9 12.6 %copy-start = (f32[16,1024]{1,0:T(8,128)S(1)}, f32[16,1024]{1,0:T(8,128)}, u32[]{:S(2)}) copy-start(f32[16,1024]{1,0:T(8,128)} %fusion.42) | copy-start | bytes 196612
  666.1 12.6 %copy-start.3 = (f32[16,1024]{1,0:T(8,128)S(1)}, f32[16,1024]{1,0:T(8,128)}, u32[]{:S(2)}) copy-start(f32[16,1024]{1,0:T(8,128)} %fusion.41) | copy-start | bytes 196612
Sparse Core Ops, SparseCore 0:
  9.1 86.1 all-gather.6
  111.1 85.3 all-gather.8
  212.3 85.3 all-gather.10
  381.3 79.9 all-gather.12
  477.1 85.3 all-gather.14
  578.3 85.3 all-gather.16
where the time goes:
time: 754 us
  waiting for transfers between devices  507 us (67%)
  blocking collectives  135 us (18%)
  matrix products  75.1 us (10%)
  local copies, waits for them, and re-layouts  16.4 us (2%)
  between operations  15 us (2%)
    all_gather x6, waiting for transfers between devices, apply_ham(): whole = lax.all_gather(current, ('blk', 'reader'), axis=1, tiled=True)  506 us
    psum x2, blocking collectives, shards(): squares = lax.psum(jnp.sum(third * third, axis=1), ('blk', 'reader'))  135 us
    dot_general x6, matrix products, contribute(): jnp.einsum('vkc,krc->vkr', sources, tiles, precision=lax.Precision.HIGHEST)  71.7 us
  transfers between devices with their start and end apart: 6, of which 6 were waited for; matrix products, arithmetic and copies ran while one was open for 0% of the time, Pallas kernels for 0%

commit v1 on v0

--- a/solution.py
+++ b/solution.py
@@ -19,7 +19,12 @@
     groups = tiles_here.shape[0]
     slots = tiles_here.shape[1]
     group_tiles = lax.axis_size("reader") * row_tiles
-    whole = lax.all_gather(current, ("blk", "reader"), axis=1, tiled=True)
+    whole = jnp.concatenate(
+        lax.all_to_all(
+            jnp.stack([current] * lax.axis_size(("blk", "reader"))), ("blk", "reader"), 0, 0
+        ),
+        axis=1,
+    )
     tiled = whole.reshape(local_vecs, whole.shape[1] // TILE, TILE)
     offsets = (jnp.arange(groups, dtype=jnp.int32) * group_tiles)[:, None]
     glob = (offsets + cols_here).reshape(-1)

time: 754 us -> 453 us (0.60)
  waiting for transfers between devices: 507 us -> 26.7 us
  blocking collectives: 135 us -> 290 us
  local copies, waits for them, and re-layouts: 16.4 us -> 44.3 us
  between operations: 15 us -> 2.04 us
    all_gather x6 -> x0, waiting for transfers between devices: 506 us -> none  [apply_ham(): whole = lax.all_gather(current, ('blk', 'reader'), axis=1, tiled=True)]
    all_to_all x0 -> x5, blocking collectives: none -> 161 us  [apply_ham(): lax.all_to_all(jnp.stack([current] * lax.axis_size(('blk', 'reader'))), (...]
    another operation x0 -> x18, local copies, waits for them, and re-layouts: none -> 29.6 us  [the longest x12 26 us: apply_ham(): tiled = whole.reshape(local_vecs, whole.shape[1] // TILE, TILE)]
    all_to_all x0 -> x1, waiting for transfers between devices: none -> 26.7 us  [apply_ham(): lax.all_to_all(jnp.stack([current] * lax.axis_size(('blk', 'reader'))), (...]
  transfers between devices with their start and end apart: 6 -> 1, of which waited for: 6 -> 1; matrix products, arithmetic and copies ran while one was open for 0% -> 0% of each run, Pallas kernels for 0% -> 0%
where the time goes in v1:
time: 453 us; the launch traced here: 446 us
  blocking collectives  290 us (64%)
  matrix products  75 us (17%)
  local copies, waits for them, and re-layouts  44.3 us (10%)
  waiting for transfers between devices  26.7 us (6%)
  starting transfers between devices  7.45 us (2%)
    all_to_all x5, blocking collectives, apply_ham(): lax.all_to_all(jnp.stack([current] * lax.axis_size(('blk', 'reader'))), (...  161 us
    psum x2, blocking collectives, shards(): squares = lax.psum(jnp.sum(third * third, axis=1), ('blk', 'reader'))  129 us
    dot_general x6, matrix products, contribute(): jnp.einsum('vkc,krc->vkr', sources, tiles, precision=lax.Precision.HIGHEST)  71.6 us
    all_to_all x1, waiting for transfers between devices, apply_ham(): lax.all_to_all(jnp.stack([current] * lax.axis_size(('blk', 'reader'))), (...  26.7 us
    another operation x12, local copies, waits for them, and re-layouts, apply_ham(): tiled = whole.reshape(local_vecs, whole.shape[1] // TILE, TILE)  26 us
  transfers between devices with their start and end apart: 1, of which 1 were waited for; matrix products, arithmetic and copies ran while one was open for 0% of the time, Pallas kernels for 0%

profile of v1, /device:TPU:32, one launch (start us, length us, event | category | flops | bytes accessed | tf_op | source)
XLA Modules:
  0.0 446.4 jit_solution(16376240708065938581)
XLA Ops:
  0.0 2.4 stack.12
  2.4 7.5 %all-to-all-start = ((f32[32,16,1024]{2,1,0:T(8,128)}), f32[32,16,1024]{2,1,0:T(8,128)S(1)}, u32[]{:S(2)}, u32[]{:S(2)}) async-start(f32[32,16,1024]{2,1,0:T(8,128)} %stack.12), calls=%async_computation | async-start | bytes 4194304 | tf_op jit(solution)/shard_map/all_to_all | solution.py:23
  11.2 0.0 copy-done.1
  11.2 0.1 eq.8
  11.3 0.1 squeeze.6
  11.4 0.1 add.20
  11.5 0.1 add.21
  11.6 26.7 %all-to-all-done = f32[32,16,1024]{2,1,0:T(8,128)S(1)} async-done(((f32[32,16,1024]{2,1,0:T(8,128)}), f32[32,16,1024]{2,1,0:T(8,128)S(1)}, u32[]{:S(2)}, u32[]{:S(2)}) %all-to-all-start) | async-done | bytes 2097184 | tf_op jit(solution)/shard_map/all_to_all | solution.py:23
  38.3 2.6 copy.13
  40.9 1.7 reshape_reshape.18
  42.6 2.6 copy.14
  45.1 2.2 gather_fusion
  47.4 0.0 copy-start
  47.4 12.0 %convolution_bitcast_fusion.5 = f32[16,96,128]{2,0,1:T(8,128)S(1)} fusion(f32[96,128,128]{2,1,0:T(8,128)} %bitcast.119, f32[96,16,128]{2,1,0:T(8,128)S(1)} %gather_fusion, pred[96]{0:T(512)(128)(4,1)S(1)} %get-tuple-element.10), kind=kOutput, calls=%fused_computation.11 | convolution fusion | flops 302186496 | bytes 7864416 | tf_op jit(solution)/shard_map/vkc,krc->vkr/dot_general | solution.py:11
  59.3 0.6 fusion.16
  59.9 0.0 copy-done
  59.9 0.2 stack.13
  60.2 32.6 %all_to_all.30 = f32[32,16,1024]{2,1,0:T(8,128)S(1)} all-to-all(f32[32,16,1024]{2,1,0:T(8,128)S(1)} %stack.13), channel_id=1, replica_groups=mesh['blk'=4,'reader'=8,'bulk'=8] {'blk','reader'}, dimensions={0} | all-to-all | bytes 4194304 | tf_op jit(solution)/shard_map/all_to_all | solution.py:23
  92.8 1.2 copy.16
  94.0 1.5 reshape_reshape.19
  95.5 2.8 copy.17
  98.3 0.7 gather_fusion.1
  99.0 11.9 %convolution_bitcast_fusion.4 = f32[16,96,128]{2,0,1:T(8,128)S(1)} fusion(f32[96,128,128]{2,1,0:T(8,128)} %bitcast.120, f32[96,16,128]{2,1,0:T(8,128)S(1)} %gather_fusion.1, pred[96]{0:T(512)(128)(4,1)S(1)} %get-tuple-element.10), kind=kOutput, calls=%fused_computation.10 | convolution fusion | flops 302186496 | bytes 7864416 | tf_op jit(solution)/shard_map/vkc,krc->vkr/dot_general | solution.py:11
  111.0 0.6 fusion.14
  111.6 0.2 stack.14
  111.8 32.2 %all_to_all.31 = f32[32,16,1024]{2,1,0:T(8,128)S(1)} all-to-all(f32[32,16,1024]{2,1,0:T(8,128)S(1)} %stack.14), channel_id=1, replica_groups=mesh['blk'=4,'reader'=8,'bulk'=8] {'blk','reader'}, dimensions={0} | all-to-all | bytes 4194304 | tf_op jit(solution)/shard_map/all_to_all | solution.py:23
  144.0 1.2 copy.19
  145.2 1.5 reshape_reshape.20
  146.7 2.8 copy.20
  149.5 0.7 gather_fusion.2
  150.2 11.9 %convolution_bitcast_fusion.3 = f32[16,96,128]{2,0,1:T(8,128)S(1)} fusion(f32[96,128,128]{2,1,0:T(8,128)} %bitcast.121, f32[96,16,128]{2,1,0:T(8,128)S(1)} %gather_fusion.2, pred[96]{0:T(512)(128)(4,1)S(1)} %get-tuple-element.10), kind=kOutput, calls=%fused_computation.9 | convolution fusion | flops 302186496 | bytes 7864416 | tf_op jit(solution)/shard_map/vkc,krc->vkr/dot_general | solution.py:11
  162.2 0.6 fusion.12
  162.7 0.1 multiply_reduce_fusion.1
  162.9 64.4 %psum.14 = f32[16]{0:T(128)S(1)} all-reduce(f32[16]{0:T(128)S(1)} %get-tuple-element.8), channel_id=1, replica_groups=mesh['blk'=4,'reader'=8,'bulk'=8] {'blk','reader'}, use_global_device_ids=true, to_apply=%region_1.3 | all-reduce | flops 16 | bytes 128 | tf_op jit(solution)/shard_map/psum | solution.py:54
  227.2 0.1 broadcast_divide_fusion.1
  227.3 0.2 stack.15
  227.6 31.6 %all_to_all.32 = f32[32,16,1024]{2,1,0:T(8,128)S(1)} all-to-all(f32[32,16,1024]{2,1,0:T(8,128)S(1)} %stack.15), channel_id=1, replica_groups=mesh['blk'=4,'reader'=8,'bulk'=8] {'blk','reader'}, dimensions={0} | all-to-all | bytes 4194304 | tf_op jit(solution)/shard_map/all_to_all | solution.py:23
  259.2 1.2 copy.22
  260.4 1.5 reshape_reshape.21
  261.9 2.8 copy.23
  264.8 0.7 gather_fusion.3
  265.5 11.9 %convolution_bitcast_fusion.2 = f32[16,96,128]{2,0,1:T(8,128)S(1)} fusion(f32[96,128,128]{2,1,0:T(8,128)} %bitcast.122, f32[96,16,128]{2,1,0:T(8,128)S(1)} %gather_fusion.3, pred[96]{0:T(512)(128)(4,1)S(1)} %get-tuple-element.10), kind=kOutput, calls=%fused_computation.8 | convolution fusion | flops 302186496 | bytes 7864416 | tf_op jit(solution)/shard_map/vkc,krc->vkr/dot_general | solution.py:11
  277.4 0.6 fusion.10
  278.0 0.1 fusion.42
  278.1 0.2 stack.16
  278.3 32.2 %all_to_all.33 = f32[32,16,1024]{2,1,0:T(8,128)S(1)} all-to-all(f32[32,16,1024]{2,1,0:T(8,128)S(1)} %stack.16), channel_id=1, replica_groups=mesh['blk'=4,'reader'=8,'bulk'=8] {'blk','reader'}, dimensions={0} | all-to-all | bytes 4194304 | tf_op jit(solution)/shard_map/all_to_all | solution.py:23
  310.5 1.2 copy.25
  311.8 1.5 reshape_reshape.22
  313.3 2.8 copy.26
  316.1 0.7 gather_fusion.4
  316.8 11.9 %convolution_bitcast_fusion.1 = f32[16,96,128]{2,0,1:T(8,128)S(1)} fusion(f32[96,128,128]{2,1,0:T(8,128)} %bitcast.123, f32[96,16,128]{2,1,0:T(8,128)S(1)} %gather_fusion.4, pred[96]{0:T(512)(128)(4,1)S(1)} %get-tuple-element.10), kind=kOutput, calls=%fused_computation.7 | convolution fusion | flops 302186496 | bytes 7864416 | tf_op jit(solution)/shard_map/vkc,krc->vkr/dot_general | solution.py:11
  328.7 0.6 fusion.8
  329.3 0.1 fusion.41
  329.4 0.2 stack.17
  329.6 32.3 %all_to_all.34 = f32[32,16,1024]{2,1,0:T(8,128)S(1)} all-to-all(f32[32,16,1024]{2,1,0:T(8,128)S(1)} %stack.17), channel_id=1, replica_groups=mesh['blk'=4,'reader'=8,'bulk'=8] {'blk','reader'}, dimensions={0} | all-to-all | bytes 4194304 | tf_op jit(solution)/shard_map/all_to_all | solution.py:23
  361.9 1.2 copy.28
  363.1 1.5 reshape_reshape.23
  364.7 2.8 copy.29
  367.5 0.7 gather_fusion.5
  368.2 11.9 %convolution_bitcast_fusion = f32[16,96,128]{2,0,1:T(8,128)S(1)} fusion(f32[96,128,128]{2,1,0:T(8,128)} %bitcast.124, f32[96,16,128]{2,1,0:T(8,128)S(1)} %gather_fusion.5, pred[96]{0:T(512)(128)(4,1)S(1)} %get-tuple-element.10), kind=kOutput, calls=%fused_computation.6 | convolution fusion | flops 302186496 | bytes 7864416 | tf_op jit(solution)/shard_map/vkc,krc->vkr/dot_general | solution.py:11
  380.1 0.6 fusion.6
  380.7 0.1 multiply_reduce_fusion
  380.8 64.4 %psum.15 = f32[16]{0:T(128)S(1)} all-reduce(f32[16]{0:T(128)S(1)} %get-tuple-element.6), channel_id=1, replica_groups=mesh['blk'=4,'reader'=8,'bulk'=8] {'blk','reader'}, use_global_device_ids=true, to_apply=%region_3.5 | all-reduce | flops 16 | bytes 128 | tf_op jit(solution)/shard_map/psum | solution.py:54
  445.2 0.7 broadcast_divide_fusion
  (10 shorter events, 0.1 us)
Async XLA Ops:
  2.4 8.8 %copy-start.1 = (s32[1,4,24]{2,1,0:T(4,128)S(1)}, s32[1,4,24]{2,1,0:T(4,128)}, u32[]{:S(2)}) copy-start(s32[1,4,24]{2,1,0:T(4,128)} %param.10) | copy-start | bytes 1156
  2.4 8.9 %copy-start.2 = (s32[1,4,24]{2,1,0:T(4,128)S(1)}, s32[1,4,24]{2,1,0:T(4,128)}, u32[]{:S(2)}) copy-start(s32[1,4,24]{2,1,0:T(4,128)} %param.11) | copy-start | bytes 1156
  2.4 35.8 %all-to-all-start = ((f32[32,16,1024]{2,1,0:T(8,128)}), f32[32,16,1024]{2,1,0:T(8,128)S(1)}, u32[]{:S(2)}, u32[]{:S(2)}) async-start(f32[32,16,1024]{2,1,0:T(8,128)} %stack.12), calls=%async_computation | async-start | bytes 4194304 | tf_op jit(solution)/shard_map/all_to_all | solution.py:23
  47.4 12.6 %copy-start = (f32[16,1024]{1,0:T(8,128)S(1)}, f32[16,1024]{1,0:T(8,128)}, u32[]{:S(2)}) copy-start(f32[16,1024]{1,0:T(8,128)} %param.8) | copy-start | bytes 196612
